TPU v7x, 32 devices: a whole 2x2x4 slice. The times are simulated.
32 devices in a mesh: region: 2 (over y), tile: 4 (over z), corner: 2 (over x), kern: 2 (over core).
Axes of the slice: x: 2, y: 2, z: 4, core: 2. Of those that a mesh axis runs over, the one named last changes fastest.
Arguments:
- tile_mask: bfloat16 [16, 256, 256], P(('region', 'tile')), parts along dimension 0, may hold values from -1 to 1
- master_mask: bfloat16 [8, 256, 256], P(('region', 'tile')), parts along dimension 0, may hold values from -1 to 1
- target: bfloat16 [16, 256, 256], P(('region', 'tile')), parts along dimension 0, may hold values from 0 to 1
- inst_master: int32 [16], P(('region', 'tile')), parts along dimension 0, may hold values from 0 to 3, as said below
- inst_shift: int32 [16, 2], P(('region', 'tile')), parts along dimension 0, may hold values from 0 to 255
- kernels: float32 [2, 12, 2, 32, 32], P('corner'), may hold values from -24 to 24
- kernel_weight: float32 [2, 12], P('corner'), may hold values from 0.05 to 1
- corner_dose: float32 [2], P('corner'), may hold values from 0.6 to 1.6
Outputs:
- tile_grad: float32 [16, 256, 256], P(('region', 'tile')), parts along dimension 0
- master_grad: float32 [8, 256, 256], P(('region', 'tile')), parts along dimension 0
There are 2 independent parts, one for each index of `region`. A program takes and returns all parts, laid end to end along the dimension named above; an argument that names none is the same for every part. Nothing has to cross between parts.
Inputs may be any that keep to these rules, and one draw needn't show every extreme that they name: `inst_master`: each master cell is placed in exactly 2 tiles.
All inputs are finite; a program needn't handle non-finite values.
Results may differ from a plain program's by a relative error of at most 0.0003.
Values may be sent and summed in bfloat16 or wider, within the bound.
No kernel may reach another device: no remote copies, remote signals or barrier semaphores. Data moves between devices by JAX's collectives and lax.ppermute only.
A program may use at most 64 MiB of HBM per device.

v0:
```python
import math
import numpy as np
import jax
import jax.numpy as jnp
from jax import lax
from jax.sharding import PartitionSpec as P

P_SIZE = 256
B = 32
precise = lax.Precision.HIGHEST
steepness = 3.0
threshold = 1.0


def band_tables():
    freq = np.arange(B, dtype=np.int64) - B // 2
    pixel = np.arange(P_SIZE, dtype=np.int64)
    angle = (
        2.0 * math.pi / P_SIZE * np.mod(freq[:, None] * pixel[None, :], P_SIZE).astype(np.float64)
    )
    return (jnp.asarray(np.cos(angle), jnp.float32), jnp.asarray(-np.sin(angle), jnp.float32))


def phase_ramp(shift):
    freq = jnp.arange(B, dtype=jnp.int32) - B // 2
    total = (
        freq[None, :, None] * shift[:, 0][:, None, None]
        + freq[None, None, :] * shift[:, 1][:, None, None]
    )
    angle = 2.0 * math.pi / P_SIZE * jnp.mod(total, P_SIZE).astype(jnp.float32)
    return (jnp.cos(angle), -jnp.sin(angle))


def spectra(masks, cos_tab, sin_tab):
    rows_re = jnp.einsum("bx,nxy->nby", cos_tab, masks, precision=precise)
    rows_im = jnp.einsum("bx,nxy->nby", sin_tab, masks, precision=precise)
    spec_re = jnp.einsum("nby,cy->nbc", rows_re, cos_tab, precision=precise) - jnp.einsum(
        "nby,cy->nbc", rows_im, sin_tab, precision=precise
    )
    spec_im = jnp.einsum("nby,cy->nbc", rows_re, sin_tab, precision=precise) + jnp.einsum(
        "nby,cy->nbc", rows_im, cos_tab, precision=precise
    )
    return (spec_re, spec_im)


def back_pixels(x_re, x_im, cos_tab, sin_tab):
    half_re = jnp.einsum("bx,nbc->nxc", cos_tab, x_re, precision=precise) + jnp.einsum(
        "bx,nbc->nxc", sin_tab, x_im, precision=precise
    )
    half_im = jnp.einsum("bx,nbc->nxc", cos_tab, x_im, precision=precise) - jnp.einsum(
        "bx,nbc->nxc", sin_tab, x_re, precision=precise
    )
    return jnp.einsum("nxc,cy->nxy", half_re, cos_tab, precision=precise) + jnp.einsum(
        "nxc,cy->nxy", half_im, sin_tab, precision=precise
    )


def on_device(
    tile_mask, master_mask, target, inst_master, inst_shift, kernels, kernel_weight, corner_dose
):
    cos_tab, sin_tab = band_tables()
    scale = 1.0 / (P_SIZE * P_SIZE)
    local_tiles = tile_mask.shape[0]
    local_masters = master_mask.shape[0]
    tile_count = lax.axis_size("tile")
    tile_pos = lax.axis_index("tile")
    kern_count = lax.axis_size("kern")
    kern_pos = lax.axis_index("kern")
    per_dev = local_tiles // kern_count
    first = kern_pos * per_dev
    region_tiles = tile_count * local_tiles
    region_masters = tile_count * local_masters
    with jax.named_scope("master_spectra"):
        own_re, own_im = spectra(master_mask.astype(jnp.float32), cos_tab, sin_tab)
        own = jnp.stack([own_re, own_im], axis=1)
        every = lax.all_gather(own, "tile", axis=0, tiled=True)
    with jax.named_scope("tile_spectra"):
        mine_mask = lax.dynamic_slice_in_dim(tile_mask, first, per_dev, 0)
        goal = lax.dynamic_slice_in_dim(target, first, per_dev, 0).astype(jnp.float32)
        mine_master = lax.dynamic_slice_in_dim(inst_master, first, per_dev, 0)
        mine_shift = lax.dynamic_slice_in_dim(inst_shift, first, per_dev, 0)
        tile_re, tile_im = spectra(mine_mask.astype(jnp.float32), cos_tab, sin_tab)
        ph_re, ph_im = phase_ramp(mine_shift)
        pick = (
            mine_master[:, None] == jnp.arange(region_masters, dtype=jnp.int32)[None, :]
        ).astype(jnp.float32)
        sel = jnp.sum(pick[:, :, None, None, None] * every[None], axis=1)
        sel_re = sel[:, 0]
        sel_im = sel[:, 1]
        spec_re = tile_re + (ph_re * sel_re - ph_im * sel_im)
        spec_im = tile_im + (ph_re * sel_im + ph_im * sel_re)
    dose = corner_dose[0]
    h_re = kernels[0, :, 0]
    h_im = kernels[0, :, 1]
    weights = kernel_weight[0]
    with jax.named_scope("forward_fields"):
        x_re = h_re[:, None] * spec_re[None] - h_im[:, None] * spec_im[None]
        x_im = h_re[:, None] * spec_im[None] + h_im[:, None] * spec_re[None]
        half_re = jnp.einsum("bx,knbc->knxc", cos_tab, x_re, precision=precise) + jnp.einsum(
            "bx,knbc->knxc", sin_tab, x_im, precision=precise
        )
        half_im = jnp.einsum("bx,knbc->knxc", cos_tab, x_im, precision=precise) - jnp.einsum(
            "bx,knbc->knxc", sin_tab, x_re, precision=precise
        )
        f_re = (
            jnp.einsum("knxc,cy->knxy", half_re, cos_tab, precision=precise)
            + jnp.einsum("knxc,cy->knxy", half_im, sin_tab, precision=precise)
        ) * scale
        f_im = (
            jnp.einsum("knxc,cy->knxy", half_im, cos_tab, precision=precise)
            - jnp.einsum("knxc,cy->knxy", half_re, sin_tab, precision=precise)
        ) * scale
    with jax.named_scope("resist_sensitivity"):
        intensity = jnp.sum(weights[:, None, None, None] * (f_re * f_re + f_im * f_im), axis=0)
        resist = jax.nn.sigmoid(steepness * (dose * intensity - threshold))
        sens = 2.0 * (resist - goal) * resist * (1.0 - resist) * steepness * dose
    with jax.named_scope("adjoint_spectra"):
        g_re = (2.0 * weights)[:, None, None, None] * sens[None] * f_re
        g_im = (2.0 * weights)[:, None, None, None] * sens[None] * f_im
        mid_re = jnp.einsum("knxy,cy->knxc", g_re, cos_tab, precision=precise) - jnp.einsum(
            "knxy,cy->knxc", g_im, sin_tab, precision=precise
        )
        mid_im = jnp.einsum("knxy,cy->knxc", g_re, sin_tab, precision=precise) + jnp.einsum(
            "knxy,cy->knxc", g_im, cos_tab, precision=precise
        )
        out_re = (
            jnp.einsum("bx,knxc->knbc", cos_tab, mid_re, precision=precise)
            - jnp.einsum("bx,knxc->knbc", sin_tab, mid_im, precision=precise)
        ) * scale
        out_im = (
            jnp.einsum("bx,knxc->knbc", cos_tab, mid_im, precision=precise)
            + jnp.einsum("bx,knxc->knbc", sin_tab, mid_re, precision=precise)
        ) * scale
        grad_re = jnp.sum(h_re[:, None] * out_re + h_im[:, None] * out_im, axis=0)
        grad_im = jnp.sum(h_re[:, None] * out_im - h_im[:, None] * out_re, axis=0)
    with jax.named_scope("gradient_exchange"):
        back_re = ph_re * grad_re + ph_im * grad_im
        back_im = ph_re * grad_im - ph_im * grad_re
        tile_slot = tile_pos * local_tiles + first + jnp.arange(per_dev, dtype=jnp.int32)
        tile_pick = (
            tile_slot[:, None] == jnp.arange(region_tiles, dtype=jnp.int32)[None, :]
        ).astype(jnp.float32)
        own_grad = jnp.stack([grad_re, grad_im], axis=1)
        own_back = jnp.stack([back_re, back_im], axis=1)
        tile_part = jnp.sum(tile_pick[:, :, None, None, None] * own_grad[:, None], axis=0)
        master_part = jnp.sum(pick[:, :, None, None, None] * own_back[:, None], axis=0)
        slots = jnp.concatenate([tile_part, master_part], axis=0)
        summed = lax.psum(slots, ("tile", "corner", "kern"))
        mine_tiles = lax.dynamic_slice_in_dim(summed, tile_pos * local_tiles, local_tiles, 0)
        mine_masters = lax.dynamic_slice_in_dim(
            summed, region_tiles + tile_pos * local_masters, local_masters, 0
        )
    with jax.named_scope("pixel_gradients"):
        tile_grad = back_pixels(mine_tiles[:, 0], mine_tiles[:, 1], cos_tab, sin_tab)
        master_grad = back_pixels(mine_masters[:, 0], mine_masters[:, 1], cos_tab, sin_tab)
    return (tile_grad, master_grad)


def solution(mesh):
    return jax.shard_map(
        on_device,
        mesh=mesh,
        in_specs=(
            P(("region", "tile"), None, None),
            P(("region", "tile"), None, None),
            P(("region", "tile"), None, None),
            P(("region", "tile")),
            P(("region", "tile"), None),
            P("corner", None, None, None, None),
            P("corner", None),
            P("corner"),
        ),
        out_specs=(P(("region", "tile"), None, None), P(("region", "tile"), None, None)),
        check_vma=False,
    )
```

profile of v0, /device:TPU:0, one launch (start us, length us, event | category | flops | bytes accessed | tf_op | source)
XLA Modules:
  0.0 185.2 jit_solution(1260496238623281663)
XLA Ops:
  7.3 1.1 fusion.41
  8.4 1.1 fusion.39
  11.4 1.0 convolution_bitcast_fusion.1
  12.4 1.0 convolution_bitcast_fusion
  16.5 1.3 dynamic_slice.20
  20.4 15.1 %all_gather.3 = f32[4,2,32,32]{3,2,1,0:T(8,128)S(1)} all-gather(f32[1,2,32,32]{3,2,1,0:T(8,128)S(1)} %pad_maximum_fusion.1), channel_id=1, replica_groups=mesh['region'=2,'tile'=4,'corner'=2,'kern'=2] {'tile'}, dimensions={0}, use_global_device_ids=true | all-gather | bytes 40960 | tf_op jit(solution)/shard_map/master_spectra/all_gather | solution.py:76
  35.4 1.3 fusion.75
  38.8 1.1 fusion.77
  42.0 2.7 %fusion.83 = f32[12,256,256]{2,1,0:T(8,128)S(1)} fusion(f32[12,256,32]{1,2,0:T(8,128)S(1)} %fusion.15, f32[32,256,1]{1,0,2:T(8,128)S(1)} %copy-done.6), kind=kOutput, calls=%fused_computation.143 | convolution fusion | flops 301989888 | bytes 3571712 | tf_op jit(solution)/shard_map/forward_fields/knxc,cy->knxy/dot_general | solution.py:106
  44.8 4.3 %fusion.84 = f32[12,256,256]{2,1,0:T(8,128)} fusion(f32[12,256,32]{1,2,0:T(8,128)S(1)} %fusion.14, f32[32,256,1]{1,0,2:T(8,128)S(1)} %copy-done.6), kind=kOutput, calls=%fused_computation.144 | convolution fusion | flops 301989888 | bytes 3571712 | tf_op jit(solution)/shard_map/forward_fields/knxc,cy->knxy/dot_general | solution.py:110
  49.1 2.7 %add_multiply_fusion = f32[12,256,256]{2,1,0:T(8,128)S(1)} fusion(f32[12,256,256]{2,1,0:T(8,128)S(1)} %fusion.83, f32[12,256,32]{1,2,0:T(8,128)S(1)} %fusion.14, f32[32,256,1]{1,0,2:T(8,128)S(1)} %copy-done.5), kind=kOutput, calls=%fused_computation.4 | convolution fusion | flops 303562752 | bytes 6717440 | tf_op jit(solution)/shard_map/forward_fields/knxc,cy->knxy/dot_general | solution.py:107
  52.5 5.6 %multiply_reduce_fusion = (f32[256,256]{1,0:T(8,128)S(1)}, f32[12,256,256]{2,1,0:T(8,128)S(1)}) fusion(f32[12,256,256]{2,1,0:T(8,128)S(1)} %add_multiply_fusion, f32[12]{0:T(128)S(1)} %bitcast.235, f32[12,256,256]{2,1,0:T(8,128)} %fusion.84, f32[12,256,32]{1,2,0:T(8,128)} %copy-done.7, f32[32,256,1]{1,0,2:T(8,128)S(1)} %copy-done.5), kind=kOutput, calls=%fused_computation.2 | convolution fusion | flops 307429376 | bytes 10125360 | tf_op jit(solution)/shard_map/forward_fields/knxc,cy->knxy/dot_general | solution.py:111
  58.3 3.3 %fusion = f32[12,256,32]{1,2,0:T(8,128)S(1)} fusion(f32[32,256,1]{1,0,2:T(8,128)S(1)} %copy-done.5, f32[12,256,256]{2,1,0:T(8,128)S(1)} %add_multiply_fusion, f32[256,256]{1,0:T(8,128)S(1)} %fusion.32, f32[12]{0:T(128)S(1)} %broadcast_multiply_fusion.2), kind=kOutput, calls=%fused_computation.5 | convolution fusion | flops 303562752 | bytes 3833904 | tf_op jit(solution)/shard_map/adjoint_spectra/knxy,cy->knxc/dot_general | solution.py:123
  61.6 3.3 %fusion.1 = f32[12,256,32]{1,2,0:T(8,128)S(1)} fusion(f32[32,256,1]{1,0,2:T(8,128)S(1)} %copy-done.6, f32[12,256,256]{2,1,0:T(8,128)S(1)} %add_multiply_fusion, f32[256,256]{1,0:T(8,128)S(1)} %fusion.32, f32[12]{0:T(128)S(1)} %broadcast_multiply_fusion.2), kind=kOutput, calls=%fused_computation.6 | convolution fusion | flops 303562752 | bytes 3833904 | tf_op jit(solution)/shard_map/adjoint_spectra/knxy,cy->knxc/dot_general | solution.py:120
  64.8 3.3 %fusion.13 = f32[12,256,32]{1,2,0:T(8,128)S(1)} fusion(f32[12,256,32]{1,2,0:T(8,128)S(1)} %fusion, f32[32,256,1]{1,0,2:T(8,128)S(1)} %copy-done.6, f32[12,256,256]{2,1,0:T(8,128)S(1)} %get-tuple-element.11, f32[256,256]{1,0:T(8,128)S(1)} %fusion.32, f32[12]{0:T(128)S(1)} %broadcast_multiply_fusion.2), kind=kOutput, calls=%fused_computation.19 | convolution fusion | flops 303661056 | bytes 4227120 | tf_op jit(solution)/shard_map/adjoint_spectra/knxy,cy->knxc/dot_general | solution.py:123
  68.2 3.5 %fusion.12 = f32[12,256,32]{1,2,0:T(8,128)S(1)} fusion(f32[12,256,32]{1,2,0:T(8,128)S(1)} %fusion.1, f32[32,256,1]{1,0,2:T(8,128)S(1)} %copy-done.5, f32[12,256,256]{2,1,0:T(8,128)S(1)} %get-tuple-element.11, f32[256,256]{1,0:T(8,128)S(1)} %fusion.32, f32[12]{0:T(128)S(1)} %broadcast_multiply_fusion.2), kind=kOutput, calls=%fused_computation.18 | convolution fusion | flops 303661056 | bytes 4227120 | tf_op jit(solution)/shard_map/adjoint_spectra/knxy,cy->knxc/dot_general | solution.py:120
  74.9 91.9 %all-reduce.2.cloned.1.call-done = f32[12,2,32,32]{3,2,1,0:T(8,128)} async-done(((f32[12,2,32,32]{3,2,1,0:T(8,128)}), f32[12,2,32,32]{3,2,1,0:T(8,128)}) %all-reduce.2.cloned.1.call-update) | async-done | bytes 98320 | tf_op jit(solution)/shard_map/gradient_exchange/psum | solution.py:148
  167.8 0.9 fusion.24
  169.2 1.0 fusion.53
  170.2 1.0 fusion.22
  173.7 1.1 fusion.16
  174.9 1.0 fusion.54
  175.9 1.0 fusion.21
  176.9 1.4 convolution_add_fusion
  (67 shorter events, 18.8 us)
Async XLA Ops:
  7.2 4.2 %copy-start = (bf16[2,256,256]{2,1,0:T(8,128)(2,1)S(1)}, bf16[2,256,256]{2,1,0:T(8,128)(2,1)}, u32[]{:S(2)}) copy-start(bf16[2,256,256]{2,1,0:T(8,128)(2,1)} %param.10) | copy-start | bytes 786436
  7.2 33.0 %copy-start.6 = (f32[32,256,1]{1,0,2:T(8,128)S(1)}, f32[32,256,1]{1,0,2:T(8,128)}, u32[]{:S(2)}) copy-start(f32[32,256,1]{1,0,2:T(8,128)} %constant.68) | copy-start | bytes 98308
  7.2 33.9 %copy-start.5 = (f32[32,256,1]{1,0,2:T(8,128)S(1)}, f32[32,256,1]{1,0,2:T(8,128)}, u32[]{:S(2)}) copy-start(f32[32,256,1]{1,0,2:T(8,128)} %constant.69) | copy-start | bytes 98308
  7.2 159.6 %all-reduce.2.cloned.1.call-start = ((), (), s32[]{:S(2)}) async-start(), calls=%async_computation | async-start | bytes 786432 | tf_op jit(solution)/shard_map/gradient_exchange/psum | solution.py:148
  40.0 4.8 %copy-start.1 = (f32[1,12,1,32,32]{3,4,1,2,0:T(8,128)}, f32[1,12,1,32,32]{3,4,1,2,0:T(8,128)S(1)}, u32[]{:S(2)}) copy-start(f32[1,12,1,32,32]{3,4,1,2,0:T(8,128)S(1)} %copy.22) | copy-start | bytes 147460
  40.1 4.6 %copy-start.3 = (f32[1,12,1,32,32]{3,4,1,2,0:T(8,128)}, f32[1,12,1,32,32]{3,4,1,2,0:T(8,128)S(1)}, u32[]{:S(2)}) copy-start(f32[1,12,1,32,32]{3,4,1,2,0:T(8,128)S(1)} %copy.23) | copy-start | bytes 147460
  42.0 2.8 %copy-start.7 = (f32[12,256,32]{1,2,0:T(8,128)}, f32[12,256,32]{1,2,0:T(8,128)S(1)}, u32[]{:S(2)}) copy-start(f32[12,256,32]{1,2,0:T(8,128)S(1)} %fusion.15) | copy-start | bytes 1179652
  49.1 3.4 %copy-start.11 = (f32[1,12]{1,0:T(1,128)S(1)}, f32[1,12]{1,0:T(1,128)}, u32[]{:S(2)}) copy-start(f32[1,12]{1,0:T(1,128)} %param.16) | copy-start | bytes 148
  52.5 5.6 %copy-start.10 = (bf16[2,256,256]{2,1,0:T(8,128)(2,1)S(1)}, bf16[2,256,256]{2,1,0:T(8,128)(2,1)}, u32[]{:S(2)}) copy-start(bf16[2,256,256]{2,1,0:T(8,128)(2,1)} %param.12) | copy-start | bytes 786436
  68.1 4.9 %copy-start.2 = (f32[1,12,1,32,32]{3,4,1,2,0:T(8,128)S(1)}, f32[1,12,1,32,32]{3,4,1,2,0:T(8,128)}, u32[]{:S(2)}) copy-start(f32[1,12,1,32,32]{3,4,1,2,0:T(8,128)} %copy-done.1) | copy-start | bytes 147460
  68.1 4.9 %copy-start.4 = (f32[1,12,1,32,32]{3,4,1,2,0:T(8,128)S(1)}, f32[1,12,1,32,32]{3,4,1,2,0:T(8,128)}, u32[]{:S(2)}) copy-start(f32[1,12,1,32,32]{3,4,1,2,0:T(8,128)} %copy-done.3) | copy-start | bytes 147460
  71.6 95.2 %copy-start.9 = (f32[32,256]{1,0:T(8,128)S(1)}, f32[32,256]{1,0:T(8,128)}, u32[]{:S(2)}) copy-start(f32[32,256]{1,0:T(8,128)} %constant.58.clone) | copy-start | bytes 98308
  71.7 96.1 %copy-start.8 = (f32[32,256]{1,0:T(8,128)S(1)}, f32[32,256]{1,0:T(8,128)}, u32[]{:S(2)}) copy-start(f32[32,256]{1,0:T(8,128)} %constant.59.clone) | copy-start | bytes 98308
Sparse Core Ops, SparseCore 0:
  75.0 91.7 all-reduce.1
where the time goes:
time: 187 us; the launch traced here: 185 us
  waiting for transfers between devices  91.9 us (49%)
  matrix products  55.3 us (30%)
  between operations  15.2 us (8%)
  blocking collectives  15.1 us (8%)
  local copies, waits for them, and re-layouts  4.24 us (2%)
  other arithmetic  3.34 us (2%)
    psum x1, waiting for transfers between devices, on_device(): summed = lax.psum(slots, ('tile', 'corner', 'kern'))  91.9 us
    all_gather x1, blocking collectives, on_device(): every = lax.all_gather(own, 'tile', axis=0, tiled=True)  15.1 us
    dot_general x1, matrix products, on_device(): jnp.einsum('knxc,cy->knxy', half_re, sin_tab, precision=precise)  5.58 us
    dot_general x1, matrix products, on_device(): jnp.einsum('knxc,cy->knxy', half_im, cos_tab, precision=precise)  4.34 us
  transfers between devices with their start and end apart: 1, of which 1 were waited for; matrix products, arithmetic and copies ran while one was open for 0% of the time, Pallas kernels for 0%

commit v1 on v0

--- a/solution.py
+++ b/solution.py
@@ -145,7 +145,7 @@
         tile_part = jnp.sum(tile_pick[:, :, None, None, None] * own_grad[:, None], axis=0)
         master_part = jnp.sum(pick[:, :, None, None, None] * own_back[:, None], axis=0)
         slots = jnp.concatenate([tile_part, master_part], axis=0)
-        summed = lax.psum(slots, ("tile", "corner", "kern"))
+        summed = jnp.sum(lax.all_gather(slots, ("tile", "corner", "kern")), axis=0)
         mine_tiles = lax.dynamic_slice_in_dim(summed, tile_pos * local_tiles, local_tiles, 0)
         mine_masters = lax.dynamic_slice_in_dim(
             summed, region_tiles + tile_pos * local_masters, local_masters, 0

time: 187 us -> 155 us (0.83)
  waiting for transfers between devices: 91.9 us -> 63.4 us
  matrix products: 55.3 us -> 49.4 us
  other arithmetic: 3.34 us -> 6.94 us
    psum x1 -> x0, waiting for transfers between devices: 91.9 us -> none  [on_device(): summed = lax.psum(slots, ('tile', 'corner', 'kern'))]
    all_gather x0 -> x1, waiting for transfers between devices: none -> 63.3 us  [on_device(): summed = jnp.sum(lax.all_gather(slots, ('tile', 'corner', 'kern')), axis=0)]
    reduce_sum x0 -> x1, other arithmetic: none -> 3.6 us  [on_device(): summed = jnp.sum(lax.all_gather(slots, ('tile', 'corner', 'kern')), axis=0)]
where the time goes in v1:
time: 155 us; the launch traced here: 154 us
  waiting for transfers between devices  63.4 us (41%)
  matrix products  49.4 us (32%)
  between operations  15.2 us (10%)
  blocking collectives  15.1 us (10%)
  other arithmetic  6.94 us (4%)
  local copies, waits for them, and re-layouts  4.23 us (3%)
    all_gather x1, waiting for transfers between devices, on_device(): summed = jnp.sum(lax.all_gather(slots, ('tile', 'corner', 'kern')), axis=0)  63.3 us
    all_gather x1, blocking collectives, on_device(): every = lax.all_gather(own, 'tile', axis=0, tiled=True)  15.1 us
    dot_general x1, matrix products, on_device(): jnp.einsum('knxc,cy->knxy', half_re, sin_tab, precision=precise)  5.59 us
    dot_general x1, matrix products, on_device(): jnp.einsum('knxc,cy->knxy', half_im, cos_tab, precision=precise)  4.34 us
    reduce_sum x1, other arithmetic, on_device(): summed = jnp.sum(lax.all_gather(slots, ('tile', 'corner', 'kern')), axis=0)  3.6 us
    dot_general x1, matrix products, on_device(): jnp.einsum('knxy,cy->knxc', g_im, sin_tab, precision=precise)  3.49 us
    dot_general x1, matrix products, on_device(): jnp.einsum('knxy,cy->knxc', g_im, cos_tab, precision=precise)  3.27 us
    dot_general x1, matrix products, on_device(): jnp.einsum('knxy,cy->knxc', g_re, cos_tab, precision=precise)  3.27 us
  transfers between devices with their start and end apart: 1, of which 1 were waited for; matrix products, arithmetic and copies ran while one was open for 0% of the time, Pallas kernels for 0%

profile of v1, /device:TPU:0, one launch (start us, length us, event | category | flops | bytes accessed | tf_op | source)
XLA Modules:
  0.0 154.3 jit_solution(9931831129123140346)
XLA Ops:
  7.3 1.1 fusion.41
  8.4 1.1 fusion.39
  11.4 1.0 convolution_bitcast_fusion.1
  12.4 1.0 convolution_bitcast_fusion
  16.5 1.3 dynamic_slice.20
  18.5 0.9 fusion.26
  19.4 0.9 fusion.27
  20.4 15.1 %all_gather.9 = f32[4,2,32,32]{3,2,1,0:T(8,128)S(1)} all-gather(f32[1,2,32,32]{3,2,1,0:T(8,128)S(1)} %pad_maximum_fusion.1), channel_id=1, replica_groups=mesh['region'=2,'tile'=4,'corner'=2,'kern'=2] {'tile'}, dimensions={0}, use_global_device_ids=true | all-gather | bytes 40960 | tf_op jit(solution)/shard_map/master_spectra/all_gather | solution.py:76
  35.4 1.3 fusion.75
  36.8 0.9 fusion.28
  37.8 0.9 fusion.25
  38.8 1.1 fusion.77
  42.0 2.7 %fusion.83 = f32[12,256,256]{2,1,0:T(8,128)S(1)} fusion(f32[12,256,32]{1,2,0:T(8,128)S(1)} %fusion.15, f32[32,256,1]{1,0,2:T(8,128)S(1)} %copy-done.6), kind=kOutput, calls=%fused_computation.143 | convolution fusion | flops 301989888 | bytes 3571712 | tf_op jit(solution)/shard_map/forward_fields/knxc,cy->knxy/dot_general | solution.py:106
  44.8 4.3 %fusion.84 = f32[12,256,256]{2,1,0:T(8,128)} fusion(f32[12,256,32]{1,2,0:T(8,128)S(1)} %fusion.14, f32[32,256,1]{1,0,2:T(8,128)S(1)} %copy-done.6), kind=kOutput, calls=%fused_computation.144 | convolution fusion | flops 301989888 | bytes 3571712 | tf_op jit(solution)/shard_map/forward_fields/knxc,cy->knxy/dot_general | solution.py:110
  49.1 2.7 %add_multiply_fusion = f32[12,256,256]{2,1,0:T(8,128)S(1)} fusion(f32[12,256,256]{2,1,0:T(8,128)S(1)} %fusion.83, f32[12,256,32]{1,2,0:T(8,128)S(1)} %fusion.14, f32[32,256,1]{1,0,2:T(8,128)S(1)} %copy-done.5), kind=kOutput, calls=%fused_computation.4 | convolution fusion | flops 303562752 | bytes 6717440 | tf_op jit(solution)/shard_map/forward_fields/knxc,cy->knxy/dot_general | solution.py:107
  52.5 5.6 %multiply_reduce_fusion = (f32[256,256]{1,0:T(8,128)S(1)}, f32[12,256,256]{2,1,0:T(8,128)S(1)}) fusion(f32[12,256,256]{2,1,0:T(8,128)S(1)} %add_multiply_fusion, f32[12]{0:T(128)S(1)} %bitcast.237, f32[12,256,256]{2,1,0:T(8,128)} %fusion.84, f32[12,256,32]{1,2,0:T(8,128)} %copy-done.7, f32[32,256,1]{1,0,2:T(8,128)S(1)} %copy-done.5), kind=kOutput, calls=%fused_computation.2 | convolution fusion | flops 307429376 | bytes 10125360 | tf_op jit(solution)/shard_map/forward_fields/knxc,cy->knxy/dot_general | solution.py:111
  58.3 3.3 %fusion = f32[12,256,32]{1,2,0:T(8,128)S(1)} fusion(f32[32,256,1]{1,0,2:T(8,128)S(1)} %copy-done.5, f32[12,256,256]{2,1,0:T(8,128)S(1)} %add_multiply_fusion, f32[256,256]{1,0:T(8,128)S(1)} %fusion.32, f32[12]{0:T(128)S(1)} %broadcast_multiply_fusion.2), kind=kOutput, calls=%fused_computation.5 | convolution fusion | flops 303562752 | bytes 3833904 | tf_op jit(solution)/shard_map/adjoint_spectra/knxy,cy->knxc/dot_general | solution.py:123
  61.6 3.3 %fusion.1 = f32[12,256,32]{1,2,0:T(8,128)S(1)} fusion(f32[32,256,1]{1,0,2:T(8,128)S(1)} %copy-done.6, f32[12,256,256]{2,1,0:T(8,128)S(1)} %add_multiply_fusion, f32[256,256]{1,0:T(8,128)S(1)} %fusion.32, f32[12]{0:T(128)S(1)} %broadcast_multiply_fusion.2), kind=kOutput, calls=%fused_computation.6 | convolution fusion | flops 303562752 | bytes 3833904 | tf_op jit(solution)/shard_map/adjoint_spectra/knxy,cy->knxc/dot_general | solution.py:120
  64.8 3.3 %fusion.13 = f32[12,256,32]{1,2,0:T(8,128)S(1)} fusion(f32[12,256,32]{1,2,0:T(8,128)S(1)} %fusion, f32[32,256,1]{1,0,2:T(8,128)S(1)} %copy-done.6, f32[12,256,256]{2,1,0:T(8,128)S(1)} %get-tuple-element.11, f32[256,256]{1,0:T(8,128)S(1)} %fusion.32, f32[12]{0:T(128)S(1)} %broadcast_multiply_fusion.2), kind=kOutput, calls=%fused_computation.19 | convolution fusion | flops 303661056 | bytes 4227120 | tf_op jit(solution)/shard_map/adjoint_spectra/knxy,cy->knxc/dot_general | solution.py:123
  68.2 3.5 %fusion.12 = f32[12,256,32]{1,2,0:T(8,128)S(1)} fusion(f32[12,256,32]{1,2,0:T(8,128)S(1)} %fusion.1, f32[32,256,1]{1,0,2:T(8,128)S(1)} %copy-done.5, f32[12,256,256]{2,1,0:T(8,128)S(1)} %get-tuple-element.11, f32[256,256]{1,0:T(8,128)S(1)} %fusion.32, f32[12]{0:T(128)S(1)} %broadcast_multiply_fusion.2), kind=kOutput, calls=%fused_computation.18 | convolution fusion | flops 303661056 | bytes 4227120 | tf_op jit(solution)/shard_map/adjoint_spectra/knxy,cy->knxc/dot_general | solution.py:120
  74.9 63.3 %all-gather.3.cloned.1.call-done = f32[192,2,32,32]{3,2,1,0:T(8,128)} async-done(((f32[12,2,32,32]{3,2,1,0:T(8,128)}), f32[192,2,32,32]{3,2,1,0:T(8,128)}) %all-gather.3.cloned.1.call-update) | async-done | bytes 1572880 | tf_op jit(solution)/shard_map/gradient_exchange/all_gather | solution.py:148
  138.2 3.6 %reduce_sum.60 = f32[12,2,32,32]{3,2,1,0:T(8,128)S(1)} reduce(f32[16,12,2,32,32]{4,3,2,1,0:T(8,128)} %bitcast.232, f32[]{:T(128)} %constant.51.clone.1), dimensions={0}, to_apply=%region_4.5 | reduce | flops 368640 | bytes 1671172 | tf_op jit(solution)/shard_map/gradient_exchange/reduce_sum | solution.py:148
  144.9 1.1 fusion.16
  146.0 1.4 convolution_add_fusion
  (68 shorter events, 14.3 us)
Async XLA Ops:
  7.2 4.2 %copy-start = (bf16[2,256,256]{2,1,0:T(8,128)(2,1)S(1)}, bf16[2,256,256]{2,1,0:T(8,128)(2,1)}, u32[]{:S(2)}) copy-start(bf16[2,256,256]{2,1,0:T(8,128)(2,1)} %param.10) | copy-start | bytes 786436
  7.2 33.0 %copy-start.6 = (f32[32,256,1]{1,0,2:T(8,128)S(1)}, f32[32,256,1]{1,0,2:T(8,128)}, u32[]{:S(2)}) copy-start(f32[32,256,1]{1,0,2:T(8,128)} %constant.68) | copy-start | bytes 98308
  7.2 33.9 %copy-start.5 = (f32[32,256,1]{1,0,2:T(8,128)S(1)}, f32[32,256,1]{1,0,2:T(8,128)}, u32[]{:S(2)}) copy-start(f32[32,256,1]{1,0,2:T(8,128)} %constant.69) | copy-start | bytes 98308
  7.2 131.0 %all-gather.3.cloned.1.call-start = ((), (), s32[]{:S(2)}) async-start(), calls=%async_computation | async-start | bytes 6684672 | tf_op jit(solution)/shard_map/gradient_exchange/all_gather | solution.py:148
  40.0 4.8 %copy-start.1 = (f32[1,12,1,32,32]{3,4,1,2,0:T(8,128)}, f32[1,12,1,32,32]{3,4,1,2,0:T(8,128)S(1)}, u32[]{:S(2)}) copy-start(f32[1,12,1,32,32]{3,4,1,2,0:T(8,128)S(1)} %copy.22) | copy-start | bytes 147460
  40.1 4.6 %copy-start.3 = (f32[1,12,1,32,32]{3,4,1,2,0:T(8,128)}, f32[1,12,1,32,32]{3,4,1,2,0:T(8,128)S(1)}, u32[]{:S(2)}) copy-start(f32[1,12,1,32,32]{3,4,1,2,0:T(8,128)S(1)} %copy.23) | copy-start | bytes 147460
  42.0 2.8 %copy-start.7 = (f32[12,256,32]{1,2,0:T(8,128)}, f32[12,256,32]{1,2,0:T(8,128)S(1)}, u32[]{:S(2)}) copy-start(f32[12,256,32]{1,2,0:T(8,128)S(1)} %fusion.15) | copy-start | bytes 1179652
  49.1 3.4 %copy-start.11 = (f32[1,12]{1,0:T(1,128)S(1)}, f32[1,12]{1,0:T(1,128)}, u32[]{:S(2)}) copy-start(f32[1,12]{1,0:T(1,128)} %param.16) | copy-start | bytes 148
  52.5 5.6 %copy-start.10 = (bf16[2,256,256]{2,1,0:T(8,128)(2,1)S(1)}, bf16[2,256,256]{2,1,0:T(8,128)(2,1)}, u32[]{:S(2)}) copy-start(bf16[2,256,256]{2,1,0:T(8,128)(2,1)} %param.12) | copy-start | bytes 786436
  68.1 4.9 %copy-start.2 = (f32[1,12,1,32,32]{3,4,1,2,0:T(8,128)S(1)}, f32[1,12,1,32,32]{3,4,1,2,0:T(8,128)}, u32[]{:S(2)}) copy-start(f32[1,12,1,32,32]{3,4,1,2,0:T(8,128)} %copy-done.1) | copy-start | bytes 147460
  68.1 4.9 %copy-start.4 = (f32[1,12,1,32,32]{3,4,1,2,0:T(8,128)S(1)}, f32[1,12,1,32,32]{3,4,1,2,0:T(8,128)}, u32[]{:S(2)}) copy-start(f32[1,12,1,32,32]{3,4,1,2,0:T(8,128)} %copy-done.3) | copy-start | bytes 147460
  138.2 3.6 %copy-start.9 = (f32[32,256]{1,0:T(8,128)S(1)}, f32[32,256]{1,0:T(8,128)}, u32[]{:S(2)}) copy-start(f32[32,256]{1,0:T(8,128)} %constant.58.clone) | copy-start | bytes 98308
  138.2 4.6 %copy-start.8 = (f32[32,256]{1,0:T(8,128)S(1)}, f32[32,256]{1,0:T(8,128)}, u32[]{:S(2)}) copy-start(f32[32,256]{1,0:T(8,128)} %constant.59.clone) | copy-start | bytes 98308
Sparse Core Ops, SparseCore 0:
  75.0 63.1 all-gather.2
